TPU v7x, 256 devices: a whole 4x4x8 slice. The times are simulated.
256 devices in a mesh: ctx: 32 (over x, z), head: 8 (over y, core).
Axes of the slice: x: 4, y: 4, z: 8, core: 2. Of those that a mesh axis runs over, the one named last changes fastest.
Arguments:
- query_in: bfloat16 [16384, 2048], P('ctx', 'head'), may hold values from -6 to 6
- key_in: bfloat16 [16384, 2048], P('ctx', 'head'), may hold values from -6 to 6
- value_in: bfloat16 [16384, 4096], P('ctx', 'head'), may hold values from -6 to 6
- query_taps: float32 [4, 2048], P(None, 'head'), may hold values from -3 to 3
- key_taps: float32 [4, 2048], P(None, 'head'), may hold values from -3 to 3
- value_taps: float32 [4, 4096], P(None, 'head'), may hold values from -3 to 3
- log_decay: float32 [32, 16384], P('head', 'ctx'), may hold values from -2 to 0
- beta_logit: float32 [32, 16384], P('head', 'ctx'), may hold values from -9 to 2
- gate_in: bfloat16 [16384, 4096], P('ctx', 'head'), may hold values from -6 to 6
- norm_gain: float32 [128], replicated, may hold values from 0.1 to 1.9
Outputs:
- core_out: bfloat16 [16384, 4096], P(('ctx', 'head'))
All inputs are finite; a program needn't handle non-finite values.
Results may differ from a plain program's by a relative error of at most 0.005.
Values may be sent and summed in bfloat16 or wider, within the bound.
No kernel may reach another device: no remote copies, remote signals or barrier semaphores. Data moves between devices by JAX's collectives and lax.ppermute only.
A program may use at most 64 MiB of HBM per device.

v0:
```python
import jax
import jax.numpy as jnp
from jax import lax
from jax.sharding import PartitionSpec as P

GROUP = 64
highest = lax.Precision.HIGHEST
norm_eps = 1e-06


def shifted(value, axis, steps):
    count = lax.axis_size(axis)
    first, last = (max(0, -steps), min(count, count - steps))
    return lax.ppermute(value, axis, [(source, source + steps) for source in range(first, last)])


def causal_conv(joined, taps, length):
    summed = jnp.zeros((length, joined.shape[1]), jnp.float32)
    for offset in range(taps.shape[0]):
        summed = summed + taps[offset] * joined[offset : offset + length].astype(jnp.float32)
    return jax.nn.silu(summed)


def unit_rows(matrix):
    return matrix * lax.rsqrt(jnp.sum(matrix * matrix, axis=-1, keepdims=True) + norm_eps)


def group_terms(query, keys, values, beta, logdecay):
    length = logdecay.shape[-1]
    cumul = jnp.cumsum(logdecay, axis=-1)
    row_ids = lax.broadcasted_iota(jnp.int32, (length, length), 0)
    col_ids = lax.broadcasted_iota(jnp.int32, (length, length), 1)
    inside = col_ids <= row_ids
    differ = cumul[..., :, None] - cumul[..., None, :]
    decay_mask = jnp.where(inside, jnp.exp(jnp.where(inside, differ, 0.0)), 0.0)
    keygram = jnp.einsum("...ik,...jk->...ij", keys, keys, precision=highest)
    strict = jnp.where(col_ids < row_ids, beta[..., :, None] * keygram * decay_mask, 0.0)
    identity_mats = jnp.broadcast_to(jnp.eye(length, dtype=jnp.float32), strict.shape)
    inverse = lax.linalg.triangular_solve(
        identity_mats + strict, identity_mats, left_side=True, lower=True, unit_diagonal=True
    )
    upd_values = jnp.einsum(
        "...ij,...jd->...id", inverse, beta[..., None] * values, precision=highest
    )
    upd_keys = jnp.einsum(
        "...ij,...jd->...id", inverse, (beta * jnp.exp(cumul))[..., None] * keys, precision=highest
    )
    scores = jnp.einsum("...ik,...jk->...ij", query, keys, precision=highest) * decay_mask
    last_log = cumul[..., -1:]
    query_decay = query * jnp.exp(cumul)[..., None]
    key_decay = keys * jnp.exp(last_log - cumul)[..., None]
    return (upd_values, upd_keys, scores, query_decay, key_decay, last_log[..., 0])


def group_step(state, terms):
    upd_values, upd_keys, scores, query_decay, key_decay, last_log = terms
    new_values = upd_values - jnp.einsum("...ik,...kd->...id", upd_keys, state, precision=highest)
    output = jnp.einsum("...ik,...kd->...id", query_decay, state, precision=highest)
    output = output + jnp.einsum("...ij,...jd->...id", scores, new_values, precision=highest)
    state = jnp.exp(last_log)[..., None, None] * state + jnp.einsum(
        "...ik,...id->...kd", key_decay, new_values, precision=highest
    )
    return (state, output)


def matmul_pair(left_mats, right_mats):
    return jnp.einsum("...ij,...jk->...ik", left_mats, right_mats, precision=highest)


def body(
    query_in,
    key_in,
    value_in,
    query_taps,
    key_taps,
    value_taps,
    log_decay,
    beta_logit,
    gate_in,
    norm_gain,
):
    head_size = norm_gain.shape[0]
    length = query_in.shape[0]
    value_heads = log_decay.shape[0]
    key_heads = query_in.shape[1] // head_size
    share_ratio = value_heads // key_heads
    rim_width = query_taps.shape[0] - 1
    groups_dev = length // GROUP
    tail_rows = shifted(
        (
            query_in[length - rim_width :],
            key_in[length - rim_width :],
            value_in[length - rim_width :],
        ),
        "ctx",
        1,
    )
    query_conv = causal_conv(jnp.concatenate([tail_rows[0], query_in], axis=0), query_taps, length)
    key_conv = causal_conv(jnp.concatenate([tail_rows[1], key_in], axis=0), key_taps, length)
    value_conv = causal_conv(jnp.concatenate([tail_rows[2], value_in], axis=0), value_taps, length)
    queries = (
        unit_rows(query_conv.reshape(length, key_heads, head_size)) * head_size ** (-0.5)
    ).astype(jnp.bfloat16)
    keys = unit_rows(key_conv.reshape(length, key_heads, head_size)).astype(jnp.bfloat16)
    values = value_conv.reshape(length, value_heads, head_size).astype(jnp.bfloat16)

    def blocked(array):
        return (
            array.astype(jnp.float32)
            .reshape(groups_dev, GROUP, array.shape[1], head_size)
            .transpose(0, 2, 1, 3)
        )

    def blocked_rates(array):
        return array.reshape(value_heads, groups_dev, GROUP).transpose(1, 0, 2)

    query_blocks = blocked(jnp.repeat(queries, share_ratio, axis=1))
    key_blocks = blocked(jnp.repeat(keys, share_ratio, axis=1))
    value_blocks = blocked(values)
    beta_blocks = blocked_rates(jax.nn.sigmoid(beta_logit))
    decay_blocks = blocked_rates(log_decay)
    terms = group_terms(query_blocks, key_blocks, value_blocks, beta_blocks, decay_blocks)
    upd_values, upd_keys, scores, query_decay, key_decay, last_log = terms
    identity_state = jnp.broadcast_to(
        jnp.eye(head_size, dtype=jnp.float32), (value_heads, head_size, head_size)
    )
    group_maps = jnp.exp(last_log)[..., None, None] * identity_state - jnp.einsum(
        "...ik,...ij->...kj", key_decay, upd_keys, precision=highest
    )
    query_effect = query_decay - matmul_pair(scores, upd_keys)

    def local_step(carry, packed):
        state, product = carry
        group, group_map = packed
        state, output = group_step(state, group)
        return ((state, matmul_pair(group_map, product)), output)

    zero_state = jnp.zeros((value_heads, head_size, head_size), jnp.float32)
    (local_state, shard_map_mat), local_out = lax.scan(
        local_step, (zero_state, identity_state), (terms, group_maps)
    )

    def chain_turn(turn, incoming_state):
        return shifted(matmul_pair(shard_map_mat, incoming_state) + local_state, "ctx", 1)

    incoming = lax.fori_loop(0, lax.axis_size("ctx") - 1, chain_turn, zero_state)

    def carried_step(state, packed):
        effect_group, group_map = packed
        return (matmul_pair(group_map, state), matmul_pair(effect_group, state))

    _, carried_out = lax.scan(carried_step, incoming, (query_effect, group_maps))
    output = (local_out + carried_out).transpose(0, 2, 1, 3).reshape(length, value_heads, head_size)
    gates = gate_in.reshape(length, value_heads, head_size).astype(jnp.float32)
    normed = (
        output
        * lax.rsqrt(jnp.mean(output * output, axis=-1, keepdims=True) + norm_eps)
        * norm_gain
        * jax.nn.silu(gates)
    )
    normed = normed.astype(jnp.bfloat16).reshape(length, value_heads * head_size)
    return lax.all_to_all(normed, "head", split_axis=0, concat_axis=1, tiled=True)


def solution(mesh):
    in_specs = (
        P("ctx", "head"),
        P("ctx", "head"),
        P("ctx", "head"),
        P(None, "head"),
        P(None, "head"),
        P(None, "head"),
        P("head", "ctx"),
        P("head", "ctx"),
        P("ctx", "head"),
        P(),
    )
    out_specs = P(("ctx", "head"), None)
    return jax.shard_map(body, mesh=mesh, in_specs=in_specs, out_specs=out_specs, check_vma=False)
```

profile of v0, /device:TPU:2, one launch (start us, length us, event | category | flops | bytes accessed | tf_op | source)
XLA Modules:
  0.0 657.1 jit_solution(1488363138327916721)
XLA Ops:
  23.5 157.3 %custom-call.3 = f32[8,4,1,64,64]{3,4,2,1,0:T(8,128)S(1)} custom-call(f32[8,4,1,64,64]{4,3,2,1,0:T(8,128)S(1)} %fusion.42), custom_call_target="InvertDiagBlocksLowerTriangular" | custom-call | tf_op jit(solution)/shard_map/triangular_solve | solution.py:39
  204.8 53.3 %while.39 = (s32[]{:T(128)}, f32[4,128,128]{2,1,0:T(8,128)S(1)}, f32[4,128,128]{2,1,0:T(8,128)S(1)}, f32[8,4,64,128]{3,2,1,0:T(8,128)S(1)}, f32[8,4]{1,0:T(8,128...) while((s32[]{:T(128)}, f32[4,128,128]{2,1,0:T(8,128)S(1)}, ...), condition=%wide.region_4.5_spmd.clone, body=%wide.region_3.4_spmd.clone.sunk | while | flops 277217280 | bytes 3804367 | solution.py:139
  258.1 357.7 %while.37 = (s32[]{:T(128)}, f32[4,128,128]{2,1,0:T(8,128)S(1)}, f32[4,128,128]{2,1,0:T(8,128)S(1)}, f32[4,128,128]{2,1,0:T(8,128)S(1)}, s32[]{:T(128)}) while((s32[]{:T(128)}, f32[4,128,128]{2,1,0:T(8,128)S(1)}, f32[4,128,128]{2,1,0:T(8,128)S(1)}, f32[4,128,128]{2,1,0:T(8,128)S(1)}, s32[]{:T(128)}) %tuple.71), condition=%wide.region_6.7_spmd, body=%wide.region_5.6_spmd.sunk | while | flops 100728832 | bytes 2097253 | solution.py:146
  283.1 8.4 %collective-permute-done = f32[4,128,128]{2,1,0:T(8,128)S(1)} collective-permute-done((f32[4,128,128]{2,1,0:T(8,128)S(1)}, f32[4,128,128]{2,1,0:T(8,128)S(1)}, u32[]{:S(2)}, u32[]{:S(2)}) %collective-permute-start) | collective-permute-done | bytes 262176 | tf_op jit(solution)/shard_map/while/body/eval_jaxpr/ppermute | solution.py:14
  293.9 8.4 %collective-permute-done = f32[4,128,128]{2,1,0:T(8,128)S(1)} collective-permute-done((f32[4,128,128]{2,1,0:T(8,128)S(1)}, f32[4,128,128]{2,1,0:T(8,128)S(1)}, u32[]{:S(2)}, u32[]{:S(2)}) %collective-permute-start) | collective-permute-done | bytes 262176 | tf_op jit(solution)/shard_map/while/body/eval_jaxpr/ppermute | solution.py:14
  304.7 8.4 %collective-permute-done = f32[4,128,128]{2,1,0:T(8,128)S(1)} collective-permute-done((f32[4,128,128]{2,1,0:T(8,128)S(1)}, f32[4,128,128]{2,1,0:T(8,128)S(1)}, u32[]{:S(2)}, u32[]{:S(2)}) %collective-permute-start) | collective-permute-done | bytes 262176 | tf_op jit(solution)/shard_map/while/body/eval_jaxpr/ppermute | solution.py:14
  315.5 9.1 %collective-permute-done = f32[4,128,128]{2,1,0:T(8,128)S(1)} collective-permute-done((f32[4,128,128]{2,1,0:T(8,128)S(1)}, f32[4,128,128]{2,1,0:T(8,128)S(1)}, u32[]{:S(2)}, u32[]{:S(2)}) %collective-permute-start) | collective-permute-done | bytes 262176 | tf_op jit(solution)/shard_map/while/body/eval_jaxpr/ppermute | solution.py:14
  326.8 10.2 %collective-permute-done = f32[4,128,128]{2,1,0:T(8,128)S(1)} collective-permute-done((f32[4,128,128]{2,1,0:T(8,128)S(1)}, f32[4,128,128]{2,1,0:T(8,128)S(1)}, u32[]{:S(2)}, u32[]{:S(2)}) %collective-permute-start) | collective-permute-done | bytes 262176 | tf_op jit(solution)/shard_map/while/body/eval_jaxpr/ppermute | solution.py:14
  339.4 11.2 %collective-permute-done = f32[4,128,128]{2,1,0:T(8,128)S(1)} collective-permute-done((f32[4,128,128]{2,1,0:T(8,128)S(1)}, f32[4,128,128]{2,1,0:T(8,128)S(1)}, u32[]{:S(2)}, u32[]{:S(2)}) %collective-permute-start) | collective-permute-done | bytes 262176 | tf_op jit(solution)/shard_map/while/body/eval_jaxpr/ppermute | solution.py:14
  352.9 10.3 %collective-permute-done = f32[4,128,128]{2,1,0:T(8,128)S(1)} collective-permute-done((f32[4,128,128]{2,1,0:T(8,128)S(1)}, f32[4,128,128]{2,1,0:T(8,128)S(1)}, u32[]{:S(2)}, u32[]{:S(2)}) %collective-permute-start) | collective-permute-done | bytes 262176 | tf_op jit(solution)/shard_map/while/body/eval_jaxpr/ppermute | solution.py:14
  365.5 9.4 %collective-permute-done = f32[4,128,128]{2,1,0:T(8,128)S(1)} collective-permute-done((f32[4,128,128]{2,1,0:T(8,128)S(1)}, f32[4,128,128]{2,1,0:T(8,128)S(1)}, u32[]{:S(2)}, u32[]{:S(2)}) %collective-permute-start) | collective-permute-done | bytes 262176 | tf_op jit(solution)/shard_map/while/body/eval_jaxpr/ppermute | solution.py:14
  377.3 8.6 %collective-permute-done = f32[4,128,128]{2,1,0:T(8,128)S(1)} collective-permute-done((f32[4,128,128]{2,1,0:T(8,128)S(1)}, f32[4,128,128]{2,1,0:T(8,128)S(1)}, u32[]{:S(2)}, u32[]{:S(2)}) %collective-permute-start) | collective-permute-done | bytes 262176 | tf_op jit(solution)/shard_map/while/body/eval_jaxpr/ppermute | solution.py:14
  420.6 8.6 %collective-permute-done = f32[4,128,128]{2,1,0:T(8,128)S(1)} collective-permute-done((f32[4,128,128]{2,1,0:T(8,128)S(1)}, f32[4,128,128]{2,1,0:T(8,128)S(1)}, u32[]{:S(2)}, u32[]{:S(2)}) %collective-permute-start) | collective-permute-done | bytes 262176 | tf_op jit(solution)/shard_map/while/body/eval_jaxpr/ppermute | solution.py:14
  431.5 9.7 %collective-permute-done = f32[4,128,128]{2,1,0:T(8,128)S(1)} collective-permute-done((f32[4,128,128]{2,1,0:T(8,128)S(1)}, f32[4,128,128]{2,1,0:T(8,128)S(1)}, u32[]{:S(2)}, u32[]{:S(2)}) %collective-permute-start) | collective-permute-done | bytes 262176 | tf_op jit(solution)/shard_map/while/body/eval_jaxpr/ppermute | solution.py:14
  443.5 10.9 %collective-permute-done = f32[4,128,128]{2,1,0:T(8,128)S(1)} collective-permute-done((f32[4,128,128]{2,1,0:T(8,128)S(1)}, f32[4,128,128]{2,1,0:T(8,128)S(1)}, u32[]{:S(2)}, u32[]{:S(2)}) %collective-permute-start) | collective-permute-done | bytes 262176 | tf_op jit(solution)/shard_map/while/body/eval_jaxpr/ppermute | solution.py:14
  456.8 10.5 %collective-permute-done = f32[4,128,128]{2,1,0:T(8,128)S(1)} collective-permute-done((f32[4,128,128]{2,1,0:T(8,128)S(1)}, f32[4,128,128]{2,1,0:T(8,128)S(1)}, u32[]{:S(2)}, u32[]{:S(2)}) %collective-permute-start) | collective-permute-done | bytes 262176 | tf_op jit(solution)/shard_map/while/body/eval_jaxpr/ppermute | solution.py:14
  469.6 9.6 %collective-permute-done = f32[4,128,128]{2,1,0:T(8,128)S(1)} collective-permute-done((f32[4,128,128]{2,1,0:T(8,128)S(1)}, f32[4,128,128]{2,1,0:T(8,128)S(1)}, u32[]{:S(2)}, u32[]{:S(2)}) %collective-permute-start) | collective-permute-done | bytes 262176 | tf_op jit(solution)/shard_map/while/body/eval_jaxpr/ppermute | solution.py:14
  481.5 8.8 %collective-permute-done = f32[4,128,128]{2,1,0:T(8,128)S(1)} collective-permute-done((f32[4,128,128]{2,1,0:T(8,128)S(1)}, f32[4,128,128]{2,1,0:T(8,128)S(1)}, u32[]{:S(2)}, u32[]{:S(2)}) %collective-permute-start) | collective-permute-done | bytes 262176 | tf_op jit(solution)/shard_map/while/body/eval_jaxpr/ppermute | solution.py:14
  535.8 9.6 %collective-permute-done = f32[4,128,128]{2,1,0:T(8,128)S(1)} collective-permute-done((f32[4,128,128]{2,1,0:T(8,128)S(1)}, f32[4,128,128]{2,1,0:T(8,128)S(1)}, u32[]{:S(2)}, u32[]{:S(2)}) %collective-permute-start) | collective-permute-done | bytes 262176 | tf_op jit(solution)/shard_map/while/body/eval_jaxpr/ppermute | solution.py:14
  547.7 10.7 %collective-permute-done = f32[4,128,128]{2,1,0:T(8,128)S(1)} collective-permute-done((f32[4,128,128]{2,1,0:T(8,128)S(1)}, f32[4,128,128]{2,1,0:T(8,128)S(1)}, u32[]{:S(2)}, u32[]{:S(2)}) %collective-permute-start) | collective-permute-done | bytes 262176 | tf_op jit(solution)/shard_map/while/body/eval_jaxpr/ppermute | solution.py:14
  560.7 10.6 %collective-permute-done = f32[4,128,128]{2,1,0:T(8,128)S(1)} collective-permute-done((f32[4,128,128]{2,1,0:T(8,128)S(1)}, f32[4,128,128]{2,1,0:T(8,128)S(1)}, u32[]{:S(2)}, u32[]{:S(2)}) %collective-permute-start) | collective-permute-done | bytes 262176 | tf_op jit(solution)/shard_map/while/body/eval_jaxpr/ppermute | solution.py:14
  573.7 9.8 %collective-permute-done = f32[4,128,128]{2,1,0:T(8,128)S(1)} collective-permute-done((f32[4,128,128]{2,1,0:T(8,128)S(1)}, f32[4,128,128]{2,1,0:T(8,128)S(1)}, u32[]{:S(2)}, u32[]{:S(2)}) %collective-permute-start) | collective-permute-done | bytes 262176 | tf_op jit(solution)/shard_map/while/body/eval_jaxpr/ppermute | solution.py:14
  615.9 21.4 %while.38 = (s32[]{:T(128)}, f32[4,128,128]{2,1,0:T(8,128)S(1)}, f32[8,4,64,128]{3,2,1,0:T(8,128)S(1)}, f32[8,4,128,128]{3,2,1,0:T(8,128)}, f32[8,4,64,128]{3,2,1,0:T(8,128)}, /*index=5*/s32[]{:T(128)}) while((s32[]{:T(128)}, f32[4,128,128]{2,1,0:T(8,128)S(1)}, f32[8,4,64,128]{3,2,1,0:T(8,128)S(1)}, f32[8,4,128,128]{3,2,1,0:T(8,128)}, ...), condition=%wide.region_8.9_spmd, body=%wide.region_7.8_spmd.sunk | while | flops 150994944 | bytes 1836113 | solution.py:152
  641.6 14.6 %all_to_all.19 = bf16[8,64,512]{2,1,0:T(8,128)(2,1)S(1)} all-to-all(bf16[8,64,512]{2,1,0:T(8,128)(2,1)S(1)} %bitcast.148), channel_id=1, replica_groups=mesh['ctx'=32,'head'=8] {'head'}, dimensions={0} | all-to-all | bytes 1048576 | tf_op jit(solution)/shard_map/all_to_all | solution.py:162
  (232 shorter events, 300.3 us)
Async XLA Ops:
  0.7 18.5 %collective-permute-start.1 = (bf16[3,256]{1,0:T(4,128)(2,1)S(1)}, bf16[3,256]{1,0:T(4,128)(2,1)S(1)}, u32[]{:S(2)}, u32[]{:S(2)}) collective-permute-start(bf16[3,256]{1,0:T(4,128)(2,1)S(1)} %slice.81), channel_id=1, source_target_pairs={{0,8},{8,16},{16,24},{24,32},{32,40},{40,48},{48,56},{56,64},{64,7... | collective-permute-start | bytes 4616 | tf_op jit(solution)/shard_map/ppermute | solution.py:14
  5.2 191.8 %collective-permute-start.2 = (bf16[3,512]{1,0:T(4,128)(2,1)S(1)}, bf16[3,512]{1,0:T(4,128)(2,1)S(1)}, u32[]{:S(2)}, u32[]{:S(2)}) collective-permute-start(bf16[3,512]{1,0:T(4,128)(2,1)S(1)} %slice.89), channel_id=1, source_target_pairs={{0,8},{8,16},{16,24},{24,32},{32,40},{40,48},{48,56},{56,64},{64,7... | collective-permute-start | bytes 9224 | tf_op jit(solution)/shard_map/ppermute | solution.py:14
  9.8 172.9 %collective-permute-start.3 = (bf16[3,256]{1,0:T(4,128)(2,1)S(1)}, bf16[3,256]{1,0:T(4,128)(2,1)S(1)}, u32[]{:S(2)}, u32[]{:S(2)}) collective-permute-start(bf16[3,256]{1,0:T(4,128)(2,1)S(1)} %slice.97), channel_id=1, source_target_pairs={{0,8},{8,16},{16,24},{24,32},{32,40},{40,48},{48,56},{56,64},{64,7... | collective-permute-start | bytes 4616 | tf_op jit(solution)/shard_map/ppermute | solution.py:14
  258.8 11.2 %collective-permute-start = (f32[4,128,128]{2,1,0:T(8,128)S(1)}, f32[4,128,128]{2,1,0:T(8,128)S(1)}, u32[]{:S(2)}, u32[]{:S(2)}) collective-permute-start(f32[4,128,128]{2,1,0:T(8,128)S(1)} %convolution_add_fusion.5), channel_id=1, source_target_pairs={{0,8},{8,16},{16,24},{24,32},{32,40},{40,48},{48,56},{56,64},{64,7... | collective-permute-start | bytes 786440 | tf_op jit(solution)/shard_map/while/body/eval_jaxpr/ppermute | solution.py:14
  270.4 10.4 %collective-permute-start = (f32[4,128,128]{2,1,0:T(8,128)S(1)}, f32[4,128,128]{2,1,0:T(8,128)S(1)}, u32[]{:S(2)}, u32[]{:S(2)}) collective-permute-start(f32[4,128,128]{2,1,0:T(8,128)S(1)} %convolution_add_fusion.5), channel_id=1, source_target_pairs={{0,8},{8,16},{16,24},{24,32},{32,40},{40,48},{48,56},{56,64},{64,7... | collective-permute-start | bytes 786440 | tf_op jit(solution)/shard_map/while/body/eval_jaxpr/ppermute | solution.py:14
  281.2 10.4 %collective-permute-start = (f32[4,128,128]{2,1,0:T(8,128)S(1)}, f32[4,128,128]{2,1,0:T(8,128)S(1)}, u32[]{:S(2)}, u32[]{:S(2)}) collective-permute-start(f32[4,128,128]{2,1,0:T(8,128)S(1)} %convolution_add_fusion.5), channel_id=1, source_target_pairs={{0,8},{8,16},{16,24},{24,32},{32,40},{40,48},{48,56},{56,64},{64,7... | collective-permute-start | bytes 786440 | tf_op jit(solution)/shard_map/while/body/eval_jaxpr/ppermute | solution.py:14
  292.0 10.4 %collective-permute-start = (f32[4,128,128]{2,1,0:T(8,128)S(1)}, f32[4,128,128]{2,1,0:T(8,128)S(1)}, u32[]{:S(2)}, u32[]{:S(2)}) collective-permute-start(f32[4,128,128]{2,1,0:T(8,128)S(1)} %convolution_add_fusion.5), channel_id=1, source_target_pairs={{0,8},{8,16},{16,24},{24,32},{32,40},{40,48},{48,56},{56,64},{64,7... | collective-permute-start | bytes 786440 | tf_op jit(solution)/shard_map/while/body/eval_jaxpr/ppermute | solution.py:14
  302.7 10.4 %collective-permute-start = (f32[4,128,128]{2,1,0:T(8,128)S(1)}, f32[4,128,128]{2,1,0:T(8,128)S(1)}, u32[]{:S(2)}, u32[]{:S(2)}) collective-permute-start(f32[4,128,128]{2,1,0:T(8,128)S(1)} %convolution_add_fusion.5), channel_id=1, source_target_pairs={{0,8},{8,16},{16,24},{24,32},{32,40},{40,48},{48,56},{56,64},{64,7... | collective-permute-start | bytes 786440 | tf_op jit(solution)/shard_map/while/body/eval_jaxpr/ppermute | solution.py:14
  313.5 11.0 %collective-permute-start = (f32[4,128,128]{2,1,0:T(8,128)S(1)}, f32[4,128,128]{2,1,0:T(8,128)S(1)}, u32[]{:S(2)}, u32[]{:S(2)}) collective-permute-start(f32[4,128,128]{2,1,0:T(8,128)S(1)} %convolution_add_fusion.5), channel_id=1, source_target_pairs={{0,8},{8,16},{16,24},{24,32},{32,40},{40,48},{48,56},{56,64},{64,7... | collective-permute-start | bytes 786440 | tf_op jit(solution)/shard_map/while/body/eval_jaxpr/ppermute | solution.py:14
  324.9 12.1 %collective-permute-start = (f32[4,128,128]{2,1,0:T(8,128)S(1)}, f32[4,128,128]{2,1,0:T(8,128)S(1)}, u32[]{:S(2)}, u32[]{:S(2)}) collective-permute-start(f32[4,128,128]{2,1,0:T(8,128)S(1)} %convolution_add_fusion.5), channel_id=1, source_target_pairs={{0,8},{8,16},{16,24},{24,32},{32,40},{40,48},{48,56},{56,64},{64,7... | collective-permute-start | bytes 786440 | tf_op jit(solution)/shard_map/while/body/eval_jaxpr/ppermute | solution.py:14
  337.4 13.1 %collective-permute-start = (f32[4,128,128]{2,1,0:T(8,128)S(1)}, f32[4,128,128]{2,1,0:T(8,128)S(1)}, u32[]{:S(2)}, u32[]{:S(2)}) collective-permute-start(f32[4,128,128]{2,1,0:T(8,128)S(1)} %convolution_add_fusion.5), channel_id=1, source_target_pairs={{0,8},{8,16},{16,24},{24,32},{32,40},{40,48},{48,56},{56,64},{64,7... | collective-permute-start | bytes 786440 | tf_op jit(solution)/shard_map/while/body/eval_jaxpr/ppermute | solution.py:14
  350.9 12.2 %collective-permute-start = (f32[4,128,128]{2,1,0:T(8,128)S(1)}, f32[4,128,128]{2,1,0:T(8,128)S(1)}, u32[]{:S(2)}, u32[]{:S(2)}) collective-permute-start(f32[4,128,128]{2,1,0:T(8,128)S(1)} %convolution_add_fusion.5), channel_id=1, source_target_pairs={{0,8},{8,16},{16,24},{24,32},{32,40},{40,48},{48,56},{56,64},{64,7... | collective-permute-start | bytes 786440 | tf_op jit(solution)/shard_map/while/body/eval_jaxpr/ppermute | solution.py:14
  363.6 11.4 %collective-permute-start = (f32[4,128,128]{2,1,0:T(8,128)S(1)}, f32[4,128,128]{2,1,0:T(8,128)S(1)}, u32[]{:S(2)}, u32[]{:S(2)}) collective-permute-start(f32[4,128,128]{2,1,0:T(8,128)S(1)} %convolution_add_fusion.5), channel_id=1, source_target_pairs={{0,8},{8,16},{16,24},{24,32},{32,40},{40,48},{48,56},{56,64},{64,7... | collective-permute-start | bytes 786440 | tf_op jit(solution)/shard_map/while/body/eval_jaxpr/ppermute | solution.py:14
  375.4 10.5 %collective-permute-start = (f32[4,128,128]{2,1,0:T(8,128)S(1)}, f32[4,128,128]{2,1,0:T(8,128)S(1)}, u32[]{:S(2)}, u32[]{:S(2)}) collective-permute-start(f32[4,128,128]{2,1,0:T(8,128)S(1)} %convolution_add_fusion.5), channel_id=1, source_target_pairs={{0,8},{8,16},{16,24},{24,32},{32,40},{40,48},{48,56},{56,64},{64,7... | collective-permute-start | bytes 786440 | tf_op jit(solution)/shard_map/while/body/eval_jaxpr/ppermute | solution.py:14
  418.6 10.5 %collective-permute-start = (f32[4,128,128]{2,1,0:T(8,128)S(1)}, f32[4,128,128]{2,1,0:T(8,128)S(1)}, u32[]{:S(2)}, u32[]{:S(2)}) collective-permute-start(f32[4,128,128]{2,1,0:T(8,128)S(1)} %convolution_add_fusion.5), channel_id=1, source_target_pairs={{0,8},{8,16},{16,24},{24,32},{32,40},{40,48},{48,56},{56,64},{64,7... | collective-permute-start | bytes 786440 | tf_op jit(solution)/shard_map/while/body/eval_jaxpr/ppermute | solution.py:14
  429.5 11.7 %collective-permute-start = (f32[4,128,128]{2,1,0:T(8,128)S(1)}, f32[4,128,128]{2,1,0:T(8,128)S(1)}, u32[]{:S(2)}, u32[]{:S(2)}) collective-permute-start(f32[4,128,128]{2,1,0:T(8,128)S(1)} %convolution_add_fusion.5), channel_id=1, source_target_pairs={{0,8},{8,16},{16,24},{24,32},{32,40},{40,48},{48,56},{56,64},{64,7... | collective-permute-start | bytes 786440 | tf_op jit(solution)/shard_map/while/body/eval_jaxpr/ppermute | solution.py:14
  441.6 12.8 %collective-permute-start = (f32[4,128,128]{2,1,0:T(8,128)S(1)}, f32[4,128,128]{2,1,0:T(8,128)S(1)}, u32[]{:S(2)}, u32[]{:S(2)}) collective-permute-start(f32[4,128,128]{2,1,0:T(8,128)S(1)} %convolution_add_fusion.5), channel_id=1, source_target_pairs={{0,8},{8,16},{16,24},{24,32},{32,40},{40,48},{48,56},{56,64},{64,7... | collective-permute-start | bytes 786440 | tf_op jit(solution)/shard_map/while/body/eval_jaxpr/ppermute | solution.py:14
  454.8 12.4 %collective-permute-start = (f32[4,128,128]{2,1,0:T(8,128)S(1)}, f32[4,128,128]{2,1,0:T(8,128)S(1)}, u32[]{:S(2)}, u32[]{:S(2)}) collective-permute-start(f32[4,128,128]{2,1,0:T(8,128)S(1)} %convolution_add_fusion.5), channel_id=1, source_target_pairs={{0,8},{8,16},{16,24},{24,32},{32,40},{40,48},{48,56},{56,64},{64,7... | collective-permute-start | bytes 786440 | tf_op jit(solution)/shard_map/while/body/eval_jaxpr/ppermute | solution.py:14
  467.6 11.6 %collective-permute-start = (f32[4,128,128]{2,1,0:T(8,128)S(1)}, f32[4,128,128]{2,1,0:T(8,128)S(1)}, u32[]{:S(2)}, u32[]{:S(2)}) collective-permute-start(f32[4,128,128]{2,1,0:T(8,128)S(1)} %convolution_add_fusion.5), channel_id=1, source_target_pairs={{0,8},{8,16},{16,24},{24,32},{32,40},{40,48},{48,56},{56,64},{64,7... | collective-permute-start | bytes 786440 | tf_op jit(solution)/shard_map/while/body/eval_jaxpr/ppermute | solution.py:14
  479.6 10.7 %collective-permute-start = (f32[4,128,128]{2,1,0:T(8,128)S(1)}, f32[4,128,128]{2,1,0:T(8,128)S(1)}, u32[]{:S(2)}, u32[]{:S(2)}) collective-permute-start(f32[4,128,128]{2,1,0:T(8,128)S(1)} %convolution_add_fusion.5), channel_id=1, source_target_pairs={{0,8},{8,16},{16,24},{24,32},{32,40},{40,48},{48,56},{56,64},{64,7... | collective-permute-start | bytes 786440 | tf_op jit(solution)/shard_map/while/body/eval_jaxpr/ppermute | solution.py:14
  533.8 11.5 %collective-permute-start = (f32[4,128,128]{2,1,0:T(8,128)S(1)}, f32[4,128,128]{2,1,0:T(8,128)S(1)}, u32[]{:S(2)}, u32[]{:S(2)}) collective-permute-start(f32[4,128,128]{2,1,0:T(8,128)S(1)} %convolution_add_fusion.5), channel_id=1, source_target_pairs={{0,8},{8,16},{16,24},{24,32},{32,40},{40,48},{48,56},{56,64},{64,7... | collective-permute-start | bytes 786440 | tf_op jit(solution)/shard_map/while/body/eval_jaxpr/ppermute | solution.py:14
  545.7 12.6 %collective-permute-start = (f32[4,128,128]{2,1,0:T(8,128)S(1)}, f32[4,128,128]{2,1,0:T(8,128)S(1)}, u32[]{:S(2)}, u32[]{:S(2)}) collective-permute-start(f32[4,128,128]{2,1,0:T(8,128)S(1)} %convolution_add_fusion.5), channel_id=1, source_target_pairs={{0,8},{8,16},{16,24},{24,32},{32,40},{40,48},{48,56},{56,64},{64,7... | collective-permute-start | bytes 786440 | tf_op jit(solution)/shard_map/while/body/eval_jaxpr/ppermute | solution.py:14
  558.8 12.6 %collective-permute-start = (f32[4,128,128]{2,1,0:T(8,128)S(1)}, f32[4,128,128]{2,1,0:T(8,128)S(1)}, u32[]{:S(2)}, u32[]{:S(2)}) collective-permute-start(f32[4,128,128]{2,1,0:T(8,128)S(1)} %convolution_add_fusion.5), channel_id=1, source_target_pairs={{0,8},{8,16},{16,24},{24,32},{32,40},{40,48},{48,56},{56,64},{64,7... | collective-permute-start | bytes 786440 | tf_op jit(solution)/shard_map/while/body/eval_jaxpr/ppermute | solution.py:14
  571.8 11.7 %collective-permute-start = (f32[4,128,128]{2,1,0:T(8,128)S(1)}, f32[4,128,128]{2,1,0:T(8,128)S(1)}, u32[]{:S(2)}, u32[]{:S(2)}) collective-permute-start(f32[4,128,128]{2,1,0:T(8,128)S(1)} %convolution_add_fusion.5), channel_id=1, source_target_pairs={{0,8},{8,16},{16,24},{24,32},{32,40},{40,48},{48,56},{56,64},{64,7... | collective-permute-start | bytes 786440 | tf_op jit(solution)/shard_map/while/body/eval_jaxpr/ppermute | solution.py:14
  (15 other events, 288.7 us)
where the time goes:
time: 660 us; the launch traced here: 657 us
  waiting for transfers between devices  281 us (43%)
  other arithmetic  169 us (26%)
  matrix products  101 us (15%)
  starting transfers between devices  75.1 us (11%)
  blocking collectives  14.6 us (2%)
  local copies, waits for them, and re-layouts  14.4 us (2%)
    ppermute x34, waiting for transfers between devices, shifted(): lax.ppermute(value, axis, [(source, source + steps) for source in range(f...  281 us
    another operation x3, other arithmetic, group_terms(): lax.linalg.triangular_solve(identity_mats + strict, identity_mats, left_s...  157 us
    ppermute x34, starting transfers between devices, shifted(): lax.ppermute(value, axis, [(source, source + steps) for source in range(f...  75.1 us
    dot_general x56, matrix products, matmul_pair(): jnp.einsum('...ij,...jk->...ik', left_mats, right_mats, precision=highest)  46.4 us
    all_to_all x1, blocking collectives, body(): lax.all_to_all(normed, 'head', split_axis=0, concat_axis=1, tiled=True)  14.6 us
  transfers between devices with their start and end apart: 34, of which 31 were waited for; matrix products, arithmetic and copies ran while one was open for 28% of the time, Pallas kernels for 0%

commit v1 on v0

--- a/solution.py
+++ b/solution.py
@@ -159,7 +159,10 @@
         * jax.nn.silu(gates)
     )
     normed = normed.astype(jnp.bfloat16).reshape(length, value_heads * head_size)
-    return lax.all_to_all(normed, "head", split_axis=0, concat_axis=1, tiled=True)
+    return jnp.concatenate(
+        lax.all_to_all(jnp.stack(jnp.split(normed, lax.axis_size("head"), axis=0)), "head", 0, 0),
+        axis=1,
+    )
 
 
 def solution(mesh):

time: 660 us -> 660 us (level)
  no operation moved by 1% of the time
where the time goes in v1:
time: 660 us; the launch traced here: 658 us
  waiting for transfers between devices  281 us (43%)
  other arithmetic  169 us (26%)
  matrix products  100 us (15%)
  starting transfers between devices  75.1 us (11%)
  local copies, waits for them, and re-layouts  15.2 us (2%)
  blocking collectives  14.6 us (2%)
    ppermute x34, waiting for transfers between devices, shifted(): lax.ppermute(value, axis, [(source, source + steps) for source in range(f...  281 us
    another operation x3, other arithmetic, group_terms(): lax.linalg.triangular_solve(identity_mats + strict, identity_mats, left_s...  157 us
    ppermute x34, starting transfers between devices, shifted(): lax.ppermute(value, axis, [(source, source + steps) for source in range(f...  75.1 us
    dot_general x56, matrix products, matmul_pair(): jnp.einsum('...ij,...jk->...ik', left_mats, right_mats, precision=highest)  46.1 us
    all_to_all x1, blocking collectives, body(): lax.all_to_all(jnp.stack(jnp.split(normed, lax.axis_size('head'), axis=0)...  14.6 us
  transfers between devices with their start and end apart: 34, of which 31 were waited for; matrix products, arithmetic and copies ran while one was open for 28% of the time, Pallas kernels for 0%

profile of v1, /device:TPU:2, one launch (start us, length us, event | category | flops | bytes accessed | tf_op | source)
XLA Modules:
  0.0 657.7 jit_solution(15784304352971215489)
XLA Ops:
  24.5 157.3 %custom-call.3 = f32[8,4,1,64,64]{3,4,2,1,0:T(8,128)S(1)} custom-call(f32[8,4,1,64,64]{4,3,2,1,0:T(8,128)S(1)} %fusion.42), custom_call_target="InvertDiagBlocksLowerTriangular" | custom-call | tf_op jit(solution)/shard_map/triangular_solve | solution.py:39
  205.9 53.2 %while.39 = (s32[]{:T(128)}, f32[4,128,128]{2,1,0:T(8,128)S(1)}, f32[4,128,128]{2,1,0:T(8,128)S(1)}, f32[8,4,64,128]{3,2,0,1:T(8,128)S(1)}, f32[8,4]{1,0:T(8,128...) while((s32[]{:T(128)}, f32[4,128,128]{2,1,0:T(8,128)S(1)}, ...), condition=%wide.region_4.5_spmd.clone, body=%wide.region_3.4_spmd.clone.sunk | while | flops 277217280 | bytes 3804367 | solution.py:139
  259.2 357.5 %while.37 = (s32[]{:T(128)}, f32[4,128,128]{2,1,0:T(8,128)S(1)}, f32[4,128,128]{2,1,0:T(8,128)S(1)}, f32[4,128,128]{2,1,0:T(8,128)S(1)}, s32[]{:T(128)}) while((s32[]{:T(128)}, f32[4,128,128]{2,1,0:T(8,128)S(1)}, f32[4,128,128]{2,1,0:T(8,128)S(1)}, f32[4,128,128]{2,1,0:T(8,128)S(1)}, s32[]{:T(128)}) %tuple.77), condition=%wide.region_6.7_spmd, body=%wide.region_5.6_spmd.sunk | while | flops 100728832 | bytes 2097253 | solution.py:146
  284.1 8.4 %collective-permute-done = f32[4,128,128]{2,1,0:T(8,128)S(1)} collective-permute-done((f32[4,128,128]{2,1,0:T(8,128)S(1)}, f32[4,128,128]{2,1,0:T(8,128)S(1)}, u32[]{:S(2)}, u32[]{:S(2)}) %collective-permute-start) | collective-permute-done | bytes 262176 | tf_op jit(solution)/shard_map/while/body/eval_jaxpr/ppermute | solution.py:14
  294.9 8.4 %collective-permute-done = f32[4,128,128]{2,1,0:T(8,128)S(1)} collective-permute-done((f32[4,128,128]{2,1,0:T(8,128)S(1)}, f32[4,128,128]{2,1,0:T(8,128)S(1)}, u32[]{:S(2)}, u32[]{:S(2)}) %collective-permute-start) | collective-permute-done | bytes 262176 | tf_op jit(solution)/shard_map/while/body/eval_jaxpr/ppermute | solution.py:14
  305.7 8.4 %collective-permute-done = f32[4,128,128]{2,1,0:T(8,128)S(1)} collective-permute-done((f32[4,128,128]{2,1,0:T(8,128)S(1)}, f32[4,128,128]{2,1,0:T(8,128)S(1)}, u32[]{:S(2)}, u32[]{:S(2)}) %collective-permute-start) | collective-permute-done | bytes 262176 | tf_op jit(solution)/shard_map/while/body/eval_jaxpr/ppermute | solution.py:14
  316.5 9.1 %collective-permute-done = f32[4,128,128]{2,1,0:T(8,128)S(1)} collective-permute-done((f32[4,128,128]{2,1,0:T(8,128)S(1)}, f32[4,128,128]{2,1,0:T(8,128)S(1)}, u32[]{:S(2)}, u32[]{:S(2)}) %collective-permute-start) | collective-permute-done | bytes 262176 | tf_op jit(solution)/shard_map/while/body/eval_jaxpr/ppermute | solution.py:14
  327.9 10.2 %collective-permute-done = f32[4,128,128]{2,1,0:T(8,128)S(1)} collective-permute-done((f32[4,128,128]{2,1,0:T(8,128)S(1)}, f32[4,128,128]{2,1,0:T(8,128)S(1)}, u32[]{:S(2)}, u32[]{:S(2)}) %collective-permute-start) | collective-permute-done | bytes 262176 | tf_op jit(solution)/shard_map/while/body/eval_jaxpr/ppermute | solution.py:14
  340.4 11.2 %collective-permute-done = f32[4,128,128]{2,1,0:T(8,128)S(1)} collective-permute-done((f32[4,128,128]{2,1,0:T(8,128)S(1)}, f32[4,128,128]{2,1,0:T(8,128)S(1)}, u32[]{:S(2)}, u32[]{:S(2)}) %collective-permute-start) | collective-permute-done | bytes 262176 | tf_op jit(solution)/shard_map/while/body/eval_jaxpr/ppermute | solution.py:14
  353.9 10.3 %collective-permute-done = f32[4,128,128]{2,1,0:T(8,128)S(1)} collective-permute-done((f32[4,128,128]{2,1,0:T(8,128)S(1)}, f32[4,128,128]{2,1,0:T(8,128)S(1)}, u32[]{:S(2)}, u32[]{:S(2)}) %collective-permute-start) | collective-permute-done | bytes 262176 | tf_op jit(solution)/shard_map/while/body/eval_jaxpr/ppermute | solution.py:14
  366.5 9.4 %collective-permute-done = f32[4,128,128]{2,1,0:T(8,128)S(1)} collective-permute-done((f32[4,128,128]{2,1,0:T(8,128)S(1)}, f32[4,128,128]{2,1,0:T(8,128)S(1)}, u32[]{:S(2)}, u32[]{:S(2)}) %collective-permute-start) | collective-permute-done | bytes 262176 | tf_op jit(solution)/shard_map/while/body/eval_jaxpr/ppermute | solution.py:14
  378.3 8.6 %collective-permute-done = f32[4,128,128]{2,1,0:T(8,128)S(1)} collective-permute-done((f32[4,128,128]{2,1,0:T(8,128)S(1)}, f32[4,128,128]{2,1,0:T(8,128)S(1)}, u32[]{:S(2)}, u32[]{:S(2)}) %collective-permute-start) | collective-permute-done | bytes 262176 | tf_op jit(solution)/shard_map/while/body/eval_jaxpr/ppermute | solution.py:14
  421.5 8.6 %collective-permute-done = f32[4,128,128]{2,1,0:T(8,128)S(1)} collective-permute-done((f32[4,128,128]{2,1,0:T(8,128)S(1)}, f32[4,128,128]{2,1,0:T(8,128)S(1)}, u32[]{:S(2)}, u32[]{:S(2)}) %collective-permute-start) | collective-permute-done | bytes 262176 | tf_op jit(solution)/shard_map/while/body/eval_jaxpr/ppermute | solution.py:14
  432.4 9.7 %collective-permute-done = f32[4,128,128]{2,1,0:T(8,128)S(1)} collective-permute-done((f32[4,128,128]{2,1,0:T(8,128)S(1)}, f32[4,128,128]{2,1,0:T(8,128)S(1)}, u32[]{:S(2)}, u32[]{:S(2)}) %collective-permute-start) | collective-permute-done | bytes 262176 | tf_op jit(solution)/shard_map/while/body/eval_jaxpr/ppermute | solution.py:14
  444.5 10.9 %collective-permute-done = f32[4,128,128]{2,1,0:T(8,128)S(1)} collective-permute-done((f32[4,128,128]{2,1,0:T(8,128)S(1)}, f32[4,128,128]{2,1,0:T(8,128)S(1)}, u32[]{:S(2)}, u32[]{:S(2)}) %collective-permute-start) | collective-permute-done | bytes 262176 | tf_op jit(solution)/shard_map/while/body/eval_jaxpr/ppermute | solution.py:14
  457.7 10.5 %collective-permute-done = f32[4,128,128]{2,1,0:T(8,128)S(1)} collective-permute-done((f32[4,128,128]{2,1,0:T(8,128)S(1)}, f32[4,128,128]{2,1,0:T(8,128)S(1)}, u32[]{:S(2)}, u32[]{:S(2)}) %collective-permute-start) | collective-permute-done | bytes 262176 | tf_op jit(solution)/shard_map/while/body/eval_jaxpr/ppermute | solution.py:14
  470.5 9.6 %collective-permute-done = f32[4,128,128]{2,1,0:T(8,128)S(1)} collective-permute-done((f32[4,128,128]{2,1,0:T(8,128)S(1)}, f32[4,128,128]{2,1,0:T(8,128)S(1)}, u32[]{:S(2)}, u32[]{:S(2)}) %collective-permute-start) | collective-permute-done | bytes 262176 | tf_op jit(solution)/shard_map/while/body/eval_jaxpr/ppermute | solution.py:14
  482.5 8.8 %collective-permute-done = f32[4,128,128]{2,1,0:T(8,128)S(1)} collective-permute-done((f32[4,128,128]{2,1,0:T(8,128)S(1)}, f32[4,128,128]{2,1,0:T(8,128)S(1)}, u32[]{:S(2)}, u32[]{:S(2)}) %collective-permute-start) | collective-permute-done | bytes 262176 | tf_op jit(solution)/shard_map/while/body/eval_jaxpr/ppermute | solution.py:14
  536.7 9.6 %collective-permute-done = f32[4,128,128]{2,1,0:T(8,128)S(1)} collective-permute-done((f32[4,128,128]{2,1,0:T(8,128)S(1)}, f32[4,128,128]{2,1,0:T(8,128)S(1)}, u32[]{:S(2)}, u32[]{:S(2)}) %collective-permute-start) | collective-permute-done | bytes 262176 | tf_op jit(solution)/shard_map/while/body/eval_jaxpr/ppermute | solution.py:14
  548.6 10.7 %collective-permute-done = f32[4,128,128]{2,1,0:T(8,128)S(1)} collective-permute-done((f32[4,128,128]{2,1,0:T(8,128)S(1)}, f32[4,128,128]{2,1,0:T(8,128)S(1)}, u32[]{:S(2)}, u32[]{:S(2)}) %collective-permute-start) | collective-permute-done | bytes 262176 | tf_op jit(solution)/shard_map/while/body/eval_jaxpr/ppermute | solution.py:14
  561.6 10.6 %collective-permute-done = f32[4,128,128]{2,1,0:T(8,128)S(1)} collective-permute-done((f32[4,128,128]{2,1,0:T(8,128)S(1)}, f32[4,128,128]{2,1,0:T(8,128)S(1)}, u32[]{:S(2)}, u32[]{:S(2)}) %collective-permute-start) | collective-permute-done | bytes 262176 | tf_op jit(solution)/shard_map/while/body/eval_jaxpr/ppermute | solution.py:14
  574.6 9.8 %collective-permute-done = f32[4,128,128]{2,1,0:T(8,128)S(1)} collective-permute-done((f32[4,128,128]{2,1,0:T(8,128)S(1)}, f32[4,128,128]{2,1,0:T(8,128)S(1)}, u32[]{:S(2)}, u32[]{:S(2)}) %collective-permute-start) | collective-permute-done | bytes 262176 | tf_op jit(solution)/shard_map/while/body/eval_jaxpr/ppermute | solution.py:14
  616.8 21.3 %while.38 = (s32[]{:T(128)}, f32[4,128,128]{2,1,0:T(8,128)S(1)}, f32[8,4,64,128]{3,2,0,1:T(8,128)S(1)}, f32[8,4,128,128]{3,2,1,0:T(8,128)}, f32[8,4,64,128]{3,2,1,0:T(8,128)}, /*index=5*/s32[]{:T(128)}) while((s32[]{:T(128)}, f32[4,128,128]{2,1,0:T(8,128)S(1)}, f32[8,4,64,128]{3,2,0,1:T(8,128)S(1)}, f32[8,4,128,128]{3,2,1,0:T(8,128)}, ...), condition=%wide.region_8.9_spmd, body=%wide.region_7.8_spmd.sunk | while | flops 150994944 | bytes 1836113 | solution.py:152
  642.3 14.6 %all_to_all.5 = bf16[8,64,512]{2,1,0:T(8,128)(2,1)S(1)} all-to-all(bf16[8,64,512]{2,1,0:T(8,128)(2,1)S(1)} %constant_dynamic-update-slice_fusion), channel_id=1, replica_groups=mesh['ctx'=32,'head'=8] {'head'}, dimensions={0} | all-to-all | bytes 1048576 | tf_op jit(solution)/shard_map/all_to_all | solution.py:163
  (256 shorter events, 300.9 us)
Async XLA Ops:
  0.8 20.9 %collective-permute-start.1 = (bf16[3,256]{1,0:T(4,128)(2,1)S(1)}, bf16[3,256]{1,0:T(4,128)(2,1)S(1)}, u32[]{:S(2)}, u32[]{:S(2)}) collective-permute-start(bf16[3,256]{1,0:T(4,128)(2,1)S(1)} %slice.89), channel_id=1, source_target_pairs={{0,8},{8,16},{16,24},{24,32},{32,40},{40,48},{48,56},{56,64},{64,7... | collective-permute-start | bytes 4616 | tf_op jit(solution)/shard_map/ppermute | solution.py:14
  5.3 192.8 %collective-permute-start.2 = (bf16[3,512]{1,0:T(4,128)(2,1)S(1)}, bf16[3,512]{1,0:T(4,128)(2,1)S(1)}, u32[]{:S(2)}, u32[]{:S(2)}) collective-permute-start(bf16[3,512]{1,0:T(4,128)(2,1)S(1)} %slice.97), channel_id=1, source_target_pairs={{0,8},{8,16},{16,24},{24,32},{32,40},{40,48},{48,56},{56,64},{64,7... | collective-permute-start | bytes 9224 | tf_op jit(solution)/shard_map/ppermute | solution.py:14
  9.8 173.8 %collective-permute-start.3 = (bf16[3,256]{1,0:T(4,128)(2,1)S(1)}, bf16[3,256]{1,0:T(4,128)(2,1)S(1)}, u32[]{:S(2)}, u32[]{:S(2)}) collective-permute-start(bf16[3,256]{1,0:T(4,128)(2,1)S(1)} %slice.105), channel_id=1, source_target_pairs={{0,8},{8,16},{16,24},{24,32},{32,40},{40,48},{48,56},{56,64},{64,7... | collective-permute-start | bytes 4616 | tf_op jit(solution)/shard_map/ppermute | solution.py:14
  259.8 11.2 %collective-permute-start = (f32[4,128,128]{2,1,0:T(8,128)S(1)}, f32[4,128,128]{2,1,0:T(8,128)S(1)}, u32[]{:S(2)}, u32[]{:S(2)}) collective-permute-start(f32[4,128,128]{2,1,0:T(8,128)S(1)} %convolution_add_fusion.5), channel_id=1, source_target_pairs={{0,8},{8,16},{16,24},{24,32},{32,40},{40,48},{48,56},{56,64},{64,7... | collective-permute-start | bytes 786440 | tf_op jit(solution)/shard_map/while/body/eval_jaxpr/ppermute | solution.py:14
  271.4 10.4 %collective-permute-start = (f32[4,128,128]{2,1,0:T(8,128)S(1)}, f32[4,128,128]{2,1,0:T(8,128)S(1)}, u32[]{:S(2)}, u32[]{:S(2)}) collective-permute-start(f32[4,128,128]{2,1,0:T(8,128)S(1)} %convolution_add_fusion.5), channel_id=1, source_target_pairs={{0,8},{8,16},{16,24},{24,32},{32,40},{40,48},{48,56},{56,64},{64,7... | collective-permute-start | bytes 786440 | tf_op jit(solution)/shard_map/while/body/eval_jaxpr/ppermute | solution.py:14
  282.2 10.4 %collective-permute-start = (f32[4,128,128]{2,1,0:T(8,128)S(1)}, f32[4,128,128]{2,1,0:T(8,128)S(1)}, u32[]{:S(2)}, u32[]{:S(2)}) collective-permute-start(f32[4,128,128]{2,1,0:T(8,128)S(1)} %convolution_add_fusion.5), channel_id=1, source_target_pairs={{0,8},{8,16},{16,24},{24,32},{32,40},{40,48},{48,56},{56,64},{64,7... | collective-permute-start | bytes 786440 | tf_op jit(solution)/shard_map/while/body/eval_jaxpr/ppermute | solution.py:14
  314.5 11.0 %collective-permute-start = (f32[4,128,128]{2,1,0:T(8,128)S(1)}, f32[4,128,128]{2,1,0:T(8,128)S(1)}, u32[]{:S(2)}, u32[]{:S(2)}) collective-permute-start(f32[4,128,128]{2,1,0:T(8,128)S(1)} %convolution_add_fusion.5), channel_id=1, source_target_pairs={{0,8},{8,16},{16,24},{24,32},{32,40},{40,48},{48,56},{56,64},{64,7... | collective-permute-start | bytes 786440 | tf_op jit(solution)/shard_map/while/body/eval_jaxpr/ppermute | solution.py:14
  325.9 12.1 %collective-permute-start = (f32[4,128,128]{2,1,0:T(8,128)S(1)}, f32[4,128,128]{2,1,0:T(8,128)S(1)}, u32[]{:S(2)}, u32[]{:S(2)}) collective-permute-start(f32[4,128,128]{2,1,0:T(8,128)S(1)} %convolution_add_fusion.5), channel_id=1, source_target_pairs={{0,8},{8,16},{16,24},{24,32},{32,40},{40,48},{48,56},{56,64},{64,7... | collective-permute-start | bytes 786440 | tf_op jit(solution)/shard_map/while/body/eval_jaxpr/ppermute | solution.py:14
  338.5 13.1 %collective-permute-start = (f32[4,128,128]{2,1,0:T(8,128)S(1)}, f32[4,128,128]{2,1,0:T(8,128)S(1)}, u32[]{:S(2)}, u32[]{:S(2)}) collective-permute-start(f32[4,128,128]{2,1,0:T(8,128)S(1)} %convolution_add_fusion.5), channel_id=1, source_target_pairs={{0,8},{8,16},{16,24},{24,32},{32,40},{40,48},{48,56},{56,64},{64,7... | collective-permute-start | bytes 786440 | tf_op jit(solution)/shard_map/while/body/eval_jaxpr/ppermute | solution.py:14
  352.0 12.2 %collective-permute-start = (f32[4,128,128]{2,1,0:T(8,128)S(1)}, f32[4,128,128]{2,1,0:T(8,128)S(1)}, u32[]{:S(2)}, u32[]{:S(2)}) collective-permute-start(f32[4,128,128]{2,1,0:T(8,128)S(1)} %convolution_add_fusion.5), channel_id=1, source_target_pairs={{0,8},{8,16},{16,24},{24,32},{32,40},{40,48},{48,56},{56,64},{64,7... | collective-permute-start | bytes 786440 | tf_op jit(solution)/shard_map/while/body/eval_jaxpr/ppermute | solution.py:14
  364.6 11.4 %collective-permute-start = (f32[4,128,128]{2,1,0:T(8,128)S(1)}, f32[4,128,128]{2,1,0:T(8,128)S(1)}, u32[]{:S(2)}, u32[]{:S(2)}) collective-permute-start(f32[4,128,128]{2,1,0:T(8,128)S(1)} %convolution_add_fusion.5), channel_id=1, source_target_pairs={{0,8},{8,16},{16,24},{24,32},{32,40},{40,48},{48,56},{56,64},{64,7... | collective-permute-start | bytes 786440 | tf_op jit(solution)/shard_map/while/body/eval_jaxpr/ppermute | solution.py:14
  376.3 10.5 %collective-permute-start = (f32[4,128,128]{2,1,0:T(8,128)S(1)}, f32[4,128,128]{2,1,0:T(8,128)S(1)}, u32[]{:S(2)}, u32[]{:S(2)}) collective-permute-start(f32[4,128,128]{2,1,0:T(8,128)S(1)} %convolution_add_fusion.5), channel_id=1, source_target_pairs={{0,8},{8,16},{16,24},{24,32},{32,40},{40,48},{48,56},{56,64},{64,7... | collective-permute-start | bytes 786440 | tf_op jit(solution)/shard_map/while/body/eval_jaxpr/ppermute | solution.py:14
  408.8 10.4 %collective-permute-start = (f32[4,128,128]{2,1,0:T(8,128)S(1)}, f32[4,128,128]{2,1,0:T(8,128)S(1)}, u32[]{:S(2)}, u32[]{:S(2)}) collective-permute-start(f32[4,128,128]{2,1,0:T(8,128)S(1)} %convolution_add_fusion.5), channel_id=1, source_target_pairs={{0,8},{8,16},{16,24},{24,32},{32,40},{40,48},{48,56},{56,64},{64,7... | collective-permute-start | bytes 786440 | tf_op jit(solution)/shard_map/while/body/eval_jaxpr/ppermute | solution.py:14
  419.6 10.5 %collective-permute-start = (f32[4,128,128]{2,1,0:T(8,128)S(1)}, f32[4,128,128]{2,1,0:T(8,128)S(1)}, u32[]{:S(2)}, u32[]{:S(2)}) collective-permute-start(f32[4,128,128]{2,1,0:T(8,128)S(1)} %convolution_add_fusion.5), channel_id=1, source_target_pairs={{0,8},{8,16},{16,24},{24,32},{32,40},{40,48},{48,56},{56,64},{64,7... | collective-permute-start | bytes 786440 | tf_op jit(solution)/shard_map/while/body/eval_jaxpr/ppermute | solution.py:14
  430.5 11.7 %collective-permute-start = (f32[4,128,128]{2,1,0:T(8,128)S(1)}, f32[4,128,128]{2,1,0:T(8,128)S(1)}, u32[]{:S(2)}, u32[]{:S(2)}) collective-permute-start(f32[4,128,128]{2,1,0:T(8,128)S(1)} %convolution_add_fusion.5), channel_id=1, source_target_pairs={{0,8},{8,16},{16,24},{24,32},{32,40},{40,48},{48,56},{56,64},{64,7... | collective-permute-start | bytes 786440 | tf_op jit(solution)/shard_map/while/body/eval_jaxpr/ppermute | solution.py:14
  442.6 12.8 %collective-permute-start = (f32[4,128,128]{2,1,0:T(8,128)S(1)}, f32[4,128,128]{2,1,0:T(8,128)S(1)}, u32[]{:S(2)}, u32[]{:S(2)}) collective-permute-start(f32[4,128,128]{2,1,0:T(8,128)S(1)} %convolution_add_fusion.5), channel_id=1, source_target_pairs={{0,8},{8,16},{16,24},{24,32},{32,40},{40,48},{48,56},{56,64},{64,7... | collective-permute-start | bytes 786440 | tf_op jit(solution)/shard_map/while/body/eval_jaxpr/ppermute | solution.py:14
  455.8 12.4 %collective-permute-start = (f32[4,128,128]{2,1,0:T(8,128)S(1)}, f32[4,128,128]{2,1,0:T(8,128)S(1)}, u32[]{:S(2)}, u32[]{:S(2)}) collective-permute-start(f32[4,128,128]{2,1,0:T(8,128)S(1)} %convolution_add_fusion.5), channel_id=1, source_target_pairs={{0,8},{8,16},{16,24},{24,32},{32,40},{40,48},{48,56},{56,64},{64,7... | collective-permute-start | bytes 786440 | tf_op jit(solution)/shard_map/while/body/eval_jaxpr/ppermute | solution.py:14
  468.6 11.5 %collective-permute-start = (f32[4,128,128]{2,1,0:T(8,128)S(1)}, f32[4,128,128]{2,1,0:T(8,128)S(1)}, u32[]{:S(2)}, u32[]{:S(2)}) collective-permute-start(f32[4,128,128]{2,1,0:T(8,128)S(1)} %convolution_add_fusion.5), channel_id=1, source_target_pairs={{0,8},{8,16},{16,24},{24,32},{32,40},{40,48},{48,56},{56,64},{64,7... | collective-permute-start | bytes 786440 | tf_op jit(solution)/shard_map/while/body/eval_jaxpr/ppermute | solution.py:14
  480.5 10.7 %collective-permute-start = (f32[4,128,128]{2,1,0:T(8,128)S(1)}, f32[4,128,128]{2,1,0:T(8,128)S(1)}, u32[]{:S(2)}, u32[]{:S(2)}) collective-permute-start(f32[4,128,128]{2,1,0:T(8,128)S(1)} %convolution_add_fusion.5), channel_id=1, source_target_pairs={{0,8},{8,16},{16,24},{24,32},{32,40},{40,48},{48,56},{56,64},{64,7... | collective-permute-start | bytes 786440 | tf_op jit(solution)/shard_map/while/body/eval_jaxpr/ppermute | solution.py:14
  534.7 11.5 %collective-permute-start = (f32[4,128,128]{2,1,0:T(8,128)S(1)}, f32[4,128,128]{2,1,0:T(8,128)S(1)}, u32[]{:S(2)}, u32[]{:S(2)}) collective-permute-start(f32[4,128,128]{2,1,0:T(8,128)S(1)} %convolution_add_fusion.5), channel_id=1, source_target_pairs={{0,8},{8,16},{16,24},{24,32},{32,40},{40,48},{48,56},{56,64},{64,7... | collective-permute-start | bytes 786440 | tf_op jit(solution)/shard_map/while/body/eval_jaxpr/ppermute | solution.py:14
  546.6 12.7 %collective-permute-start = (f32[4,128,128]{2,1,0:T(8,128)S(1)}, f32[4,128,128]{2,1,0:T(8,128)S(1)}, u32[]{:S(2)}, u32[]{:S(2)}) collective-permute-start(f32[4,128,128]{2,1,0:T(8,128)S(1)} %convolution_add_fusion.5), channel_id=1, source_target_pairs={{0,8},{8,16},{16,24},{24,32},{32,40},{40,48},{48,56},{56,64},{64,7... | collective-permute-start | bytes 786440 | tf_op jit(solution)/shard_map/while/body/eval_jaxpr/ppermute | solution.py:14
  559.7 12.6 %collective-permute-start = (f32[4,128,128]{2,1,0:T(8,128)S(1)}, f32[4,128,128]{2,1,0:T(8,128)S(1)}, u32[]{:S(2)}, u32[]{:S(2)}) collective-permute-start(f32[4,128,128]{2,1,0:T(8,128)S(1)} %convolution_add_fusion.5), channel_id=1, source_target_pairs={{0,8},{8,16},{16,24},{24,32},{32,40},{40,48},{48,56},{56,64},{64,7... | collective-permute-start | bytes 786440 | tf_op jit(solution)/shard_map/while/body/eval_jaxpr/ppermute | solution.py:14
  572.7 11.7 %collective-permute-start = (f32[4,128,128]{2,1,0:T(8,128)S(1)}, f32[4,128,128]{2,1,0:T(8,128)S(1)}, u32[]{:S(2)}, u32[]{:S(2)}) collective-permute-start(f32[4,128,128]{2,1,0:T(8,128)S(1)} %convolution_add_fusion.5), channel_id=1, source_target_pairs={{0,8},{8,16},{16,24},{24,32},{32,40},{40,48},{48,56},{56,64},{64,7... | collective-permute-start | bytes 786440 | tf_op jit(solution)/shard_map/while/body/eval_jaxpr/ppermute | solution.py:14
  606.3 10.4 %collective-permute-start = (f32[4,128,128]{2,1,0:T(8,128)S(1)}, f32[4,128,128]{2,1,0:T(8,128)S(1)}, u32[]{:S(2)}, u32[]{:S(2)}) collective-permute-start(f32[4,128,128]{2,1,0:T(8,128)S(1)} %convolution_add_fusion.5), channel_id=1, source_target_pairs={{0,8},{8,16},{16,24},{24,32},{32,40},{40,48},{48,56},{56,64},{64,7... | collective-permute-start | bytes 786440 | tf_op jit(solution)/shard_map/while/body/eval_jaxpr/ppermute | solution.py:14
  (15 other events, 290.1 us)
